TPU v7x, 128 devices: a whole 4x4x4 slice. The times are simulated.
128 devices in a mesh: dp: 2 (over core), seq: 16 (over z, x), head: 4 (over y).
Axes of the slice: x: 4, y: 4, z: 4, core: 2. Of those that a mesh axis runs over, the one named last changes fastest.
Arguments:
- queries: bfloat16 [2, 10240, 2048], P('dp', ('seq', 'head')), may hold values from -45 to 45
- key_rows: bfloat16 [2, 10240, 2048], P('dp', ('seq', 'head')), may hold values from -6 to 6
- values: bfloat16 [2, 10240, 2048], P('dp', ('seq', 'head')), may hold values from -6 to 6
- rand_blocks: int32 [160, 16, 4], P('seq', 'head'), may hold values from 0 to 159, as said below
- out_weight: bfloat16 [2048, 2048], P('head'), may hold values from -0.125 to 0.125
- cotangent: bfloat16 [2, 10240, 2048], P('dp', ('seq', 'head')), may hold values from -6 to 6
Outputs:
- layer_out: bfloat16 [2, 10240, 2048], P('dp', ('seq', 'head'))
- grad_queries: bfloat16 [2, 10240, 2048], P('dp', ('seq', 'head'))
- grad_keys: bfloat16 [2, 10240, 2048], P('dp', ('seq', 'head'))
- grad_values: bfloat16 [2, 10240, 2048], P('dp', ('seq', 'head'))
- weight_grad: float32 [2048, 2048], P('head')
Inputs may be any that keep to these rules, and one draw needn't show every extreme that they name: `rand_blocks`: key block b lies in range b // 10 of seq. Over the 10 query blocks of one index of seq and the 4 heads of one index of head, at most 15 of the listed random blocks lie in any one range of seq; in every draw, for every index of head, some range of seq receives exactly 15 of them from every index of seq.
All inputs are finite; a program needn't handle non-finite values.
Results may differ from a plain program's by a relative error of at most 0.034.
Values may be sent and summed in bfloat16 or wider, within the bound.
No kernel may reach another device: no remote copies, remote signals or barrier semaphores. Data moves between devices by JAX's collectives and lax.ppermute only.
A program may use at most 192 MiB of HBM per device.

v0:
```python
import math

import jax
import jax.numpy as jnp
from jax import lax
from jax.sharding import PartitionSpec as P

HEAD_SIZE = 128
BLOCK_TOKENS = 64


def with_halo(block, sides, width):
    for axis, dim in sides:
        count = lax.axis_size(axis)
        forward = [(i, i + 1) for i in range(count - 1)]
        backward = [(target, source) for source, target in forward]
        low = lax.ppermute(
            lax.slice_in_dim(block, block.shape[dim] - width, None, axis=dim), axis, forward
        )
        high = lax.ppermute(lax.slice_in_dim(block, 0, width, axis=dim), axis, backward)
        block = jnp.concatenate([low, block, high], axis=dim)
    return block


def broadcast_first(block, axis, radix=4):
    count = lax.axis_size(axis)
    index = lax.axis_index(axis)
    stride = 1
    while stride * radix < count:
        stride *= radix
    while stride >= 1:
        span = stride * radix
        updated = block
        for m in range(1, radix):
            pairs = [(j, j + m * stride) for j in range(0, count, span) if j + m * stride < count]
            if pairs:
                got = lax.ppermute(block, axis, pairs)
                updated = jnp.where(index % span == m * stride, got, updated)
        block = updated
        stride //= radix
    return block


def reduce_to_first(block, axis, radix=4):
    count = lax.axis_size(axis)
    stride = 1
    while stride < count:
        span = stride * radix
        total = block
        for m in range(1, radix):
            pairs = [(j + m * stride, j) for j in range(0, count, span) if j + m * stride < count]
            if pairs:
                total = total + lax.ppermute(block, axis, pairs)
        block = total
        stride *= radix
    return block


def request_slots(rand_blocks, block_count, head_count, seq_count, capacity):
    requests = jnp.transpose(rand_blocks, (0, 2, 1)).reshape(-1)
    head_of = jnp.arange(requests.shape[0], dtype=jnp.int32) % head_count
    owners = requests // block_count
    offsets = requests % block_count
    one_hot = (owners[:, None] == jnp.arange(seq_count, dtype=jnp.int32)[None, :]).astype(
        jnp.bfloat16
    )
    count = requests.shape[0]
    lower = (
        jnp.arange(count, dtype=jnp.int32)[:, None] >= jnp.arange(count, dtype=jnp.int32)[None, :]
    ).astype(jnp.bfloat16)
    running = jnp.dot(lower, one_hot, preferred_element_type=jnp.float32)
    position = jnp.sum(one_hot.astype(jnp.float32) * (running - 1.0), axis=1).astype(jnp.int32)
    return owners, position, offsets * head_count + head_of


def gather_all(block, axis, radix=4):
    count = lax.axis_size(axis)
    if count != radix * radix:
        return lax.all_gather(block, axis, axis=0, tiled=False)
    index = lax.axis_index(axis)
    for stride in (1, radix):
        place = (index // stride) % radix
        pieces = [block]
        for m in range(1, radix):
            pairs = [
                (i, i - ((i // stride) % radix) * stride + (((i // stride) % radix + m) % radix) * stride)
                for i in range(count)
            ]
            pieces.append(lax.ppermute(block, axis, pairs))
        pieces = jnp.stack(pieces)
        order = (place - jnp.arange(radix, dtype=jnp.int32)) % radix
        block = jnp.take(pieces, order, axis=0)
        if stride > 1:
            block = block.reshape((radix * radix,) + block.shape[2:])
    return block


def per_device(queries, key_rows, values, rand_blocks, out_weight, cotangent):
    block_len = BLOCK_TOKENS
    head_dim = HEAD_SIZE
    seq_count = lax.axis_size("seq")
    seq_index = lax.axis_index("seq")
    group_count = lax.axis_size("head")
    piece_len = queries.shape[1]
    width_cols = queries.shape[2] // group_count
    stacked = jnp.concatenate([queries, key_rows, values], axis=0)
    stacked = jnp.transpose(stacked.reshape(3, piece_len, group_count, width_cols), (2, 0, 1, 3))
    stacked = lax.all_to_all(stacked, "head", split_axis=0, concat_axis=0, tiled=True)
    stacked = jnp.transpose(stacked, (1, 0, 2, 3)).reshape(3, group_count * piece_len, width_cols)
    q_rows = stacked[0]
    shard_len = q_rows.shape[0]
    head_count = width_cols // head_dim
    block_count = shard_len // block_len
    rand_count = rand_blocks.shape[2]
    key_value = jnp.concatenate([stacked[1], stacked[2]], axis=1)
    padded = with_halo(key_value, (("seq", 0),), block_len)
    first_block = broadcast_first(key_value[:block_len], "seq")
    request_count = rand_blocks.shape[0] * rand_blocks.shape[1] * rand_blocks.shape[2]
    capacity = 3 * request_count // (2 * seq_count)
    owners, position, codes = request_slots(
        rand_blocks, block_count, head_count, seq_count, capacity
    )
    slot_of = owners * capacity + position
    every_block = gather_all(rand_blocks, "seq")
    all_owners, all_position, all_codes = jax.vmap(
        lambda r: request_slots(r, block_count, head_count, seq_count, capacity)
    )(every_block)
    match = (all_owners[:, :, None] == seq_index) & (
        all_position[:, :, None] == jnp.arange(capacity, dtype=jnp.int32)[None, None, :]
    )
    asked_here = jnp.sum(jnp.where(match, all_codes[:, :, None] + 1, 0), axis=1) - 1
    slot_total = seq_count * capacity
    pair_count = block_count * head_count
    asked_flat = asked_here.reshape(slot_total)
    serve_hot = (
        asked_flat[:, None] == jnp.arange(pair_count, dtype=jnp.int32)[None, :]
    ).astype(jnp.bfloat16)
    pick_hot = (
        slot_of[:, None] == jnp.arange(slot_total, dtype=jnp.int32)[None, :]
    ).astype(jnp.bfloat16)
    kv_pairs = jnp.transpose(
        key_value.reshape(block_count, block_len, 2, head_count, head_dim), (2, 0, 3, 1, 4)
    ).reshape(2, pair_count, block_len * head_dim)

    def fetch(pairs):
        served = jnp.dot(serve_hot, pairs, preferred_element_type=jnp.float32).astype(jnp.bfloat16)
        served = served.reshape(seq_count, capacity, block_len, head_dim)
        received = lax.all_to_all(served, "seq", split_axis=0, concat_axis=0, tiled=True)
        picked = jnp.dot(
            pick_hot, received.reshape(slot_total, -1), preferred_element_type=jnp.float32
        ).astype(jnp.bfloat16)
        return picked.reshape(block_count, rand_count, head_count, block_len, head_dim)

    far_keys = fetch(kv_pairs[0])
    far_vals = fetch(kv_pairs[1])
    pair_view = padded.reshape(block_count + 2, block_len, 2, head_count, head_dim)
    window_pairs = jnp.stack(
        [pair_view[:block_count], pair_view[1 : block_count + 1], pair_view[2:]], axis=1
    ).reshape(block_count, 3 * block_len, 2, head_count, head_dim)
    window_keys = window_pairs[:, :, 0]
    window_vals = window_pairs[:, :, 1]
    first_pairs = first_block.reshape(block_len, 2, head_count, head_dim)
    first_keys = first_pairs[:, 0]
    first_vals = first_pairs[:, 1]
    global_ids = seq_index * block_count + jnp.arange(block_count, dtype=jnp.int32)
    block_total = seq_count * block_count
    window_live = jnp.stack([global_ids > 0, global_ids >= 0, global_ids < block_total - 1], axis=1)
    window_mask = jnp.repeat(window_live, block_len, axis=1)[None, :, None, :]
    query_blocks = q_rows.reshape(block_count, block_len, head_count, head_dim)
    softmax_scale = 1.0 / math.sqrt(head_dim)
    score_window = (
        jnp.einsum("ibhd,ikhd->hibk", query_blocks, window_keys, preferred_element_type=jnp.float32)
        * softmax_scale
    )
    score_first = (
        jnp.einsum("ibhd,khd->hibk", query_blocks, first_keys, preferred_element_type=jnp.float32)
        * softmax_scale
    )
    score_far = (
        jnp.einsum("ibhd,irhtd->hibrt", query_blocks, far_keys, preferred_element_type=jnp.float32)
        * softmax_scale
    )
    max_window = jnp.max(jnp.where(window_mask, score_window, -jnp.inf), axis=-1, keepdims=True)
    max_first = jnp.max(score_first, axis=-1, keepdims=True)
    max_far = jnp.max(score_far, axis=(-2, -1))[..., None]
    row_max = jnp.maximum(jnp.maximum(max_window, max_first), max_far)
    weight_window = jnp.where(window_mask, jnp.exp(score_window - row_max), 0.0)
    weight_first = jnp.exp(score_first - row_max)
    weight_far = jnp.exp(score_far - row_max[..., None])
    totals = (
        jnp.sum(weight_window, axis=-1, keepdims=True)
        + jnp.sum(weight_first, axis=-1, keepdims=True)
        + jnp.sum(weight_far, axis=(-2, -1))[..., None]
    )
    mixed = jnp.einsum(
        "hibk,ikhd->ibhd",
        weight_window.astype(jnp.bfloat16),
        window_vals,
        preferred_element_type=jnp.float32,
    )
    mixed = mixed + jnp.einsum(
        "hibk,khd->ibhd",
        weight_first.astype(jnp.bfloat16),
        first_vals,
        preferred_element_type=jnp.float32,
    )
    mixed = mixed + jnp.einsum(
        "hibrt,irhtd->ibhd",
        weight_far.astype(jnp.bfloat16),
        far_vals,
        preferred_element_type=jnp.float32,
    )
    totals_rows = jnp.transpose(totals, (1, 2, 0, 3))
    attn = (mixed / totals_rows).astype(jnp.bfloat16)
    logsum = row_max + jnp.log(totals)
    attn_rows = attn.reshape(shard_len, width_cols)
    layer_out = lax.psum_scatter(
        jnp.dot(attn_rows, out_weight, preferred_element_type=jnp.float32).astype(jnp.bfloat16),
        "head",
        scatter_dimension=0,
        tiled=True,
    )[None]
    piece_flat = lax.all_gather(cotangent, "head", axis=1, tiled=True)[0]
    grad_piece = jnp.dot(piece_flat, out_weight.T, preferred_element_type=jnp.float32).astype(
        jnp.bfloat16
    )
    weight_acc = jnp.dot(attn_rows.T, piece_flat, preferred_element_type=jnp.float32)
    token_total = lax.axis_size("dp") * seq_count * shard_len
    dp_index = lax.axis_index("dp")
    half_rows = width_cols // 2
    mine = lax.dynamic_slice_in_dim(weight_acc, dp_index * half_rows, half_rows, axis=0)
    theirs = lax.dynamic_slice_in_dim(weight_acc, (1 - dp_index) * half_rows, half_rows, axis=0)
    mine = mine + lax.ppermute(theirs, "dp", [(0, 1), (1, 0)])
    mine = lax.psum(mine.astype(jnp.bfloat16), "seq").astype(jnp.float32) * (
        1.0 / math.sqrt(token_total)
    )
    other = lax.ppermute(mine, "dp", [(0, 1), (1, 0)])
    weight_grad = jnp.where(
        dp_index == 0,
        jnp.concatenate([mine, other], axis=0),
        jnp.concatenate([other, mine], axis=0),
    )
    grad_blocks = grad_piece.reshape(block_count, block_len, head_count, head_dim)
    delta_rows = jnp.sum(grad_blocks.astype(jnp.float32) * attn.astype(jnp.float32), axis=-1)
    row_delta = jnp.transpose(delta_rows, (2, 0, 1))[..., None]
    prob_window = jnp.where(window_mask, jnp.exp(score_window - logsum), 0.0)
    prob_first = jnp.exp(score_first - logsum)
    prob_far = jnp.exp(score_far - logsum[..., None])
    dprob_window = jnp.einsum(
        "ibhd,ikhd->hibk", grad_blocks, window_vals, preferred_element_type=jnp.float32
    )
    dprob_first = jnp.einsum(
        "ibhd,khd->hibk", grad_blocks, first_vals, preferred_element_type=jnp.float32
    )
    dprob_far = jnp.einsum(
        "ibhd,irhtd->hibrt", grad_blocks, far_vals, preferred_element_type=jnp.float32
    )
    dscore_window = (prob_window * (dprob_window - row_delta)).astype(jnp.bfloat16)
    dscore_first = (prob_first * (dprob_first - row_delta)).astype(jnp.bfloat16)
    dscore_far = (prob_far * (dprob_far - row_delta[..., None])).astype(jnp.bfloat16)
    grad_q = jnp.einsum(
        "hibk,ikhd->ibhd", dscore_window, window_keys, preferred_element_type=jnp.float32
    )
    grad_q = grad_q + jnp.einsum(
        "hibk,khd->ibhd", dscore_first, first_keys, preferred_element_type=jnp.float32
    )
    grad_q = grad_q + jnp.einsum(
        "hibrt,irhtd->ibhd", dscore_far, far_keys, preferred_element_type=jnp.float32
    )
    grad_q = (grad_q * softmax_scale).astype(jnp.bfloat16)
    key_window = (
        jnp.einsum(
            "hibk,ibhd->ikhd", dscore_window, query_blocks, preferred_element_type=jnp.float32
        )
        * softmax_scale
    )
    value_window = jnp.einsum(
        "hibk,ibhd->ikhd",
        prob_window.astype(jnp.bfloat16),
        grad_blocks,
        preferred_element_type=jnp.float32,
    )
    key_first = (
        jnp.einsum("hibk,ibhd->khd", dscore_first, query_blocks, preferred_element_type=jnp.float32)
        * softmax_scale
    )
    value_first = jnp.einsum(
        "hibk,ibhd->khd",
        prob_first.astype(jnp.bfloat16),
        grad_blocks,
        preferred_element_type=jnp.float32,
    )
    key_far = (
        jnp.einsum(
            "hibrt,ibhd->irhtd", dscore_far, query_blocks, preferred_element_type=jnp.float32
        )
        * softmax_scale
    )
    value_far = jnp.einsum(
        "hibrt,ibhd->irhtd",
        prob_far.astype(jnp.bfloat16),
        grad_blocks,
        preferred_element_type=jnp.float32,
    )
    window_terms = jnp.stack(
        [
            key_window.reshape(block_count, 3, block_len, head_count, head_dim),
            value_window.reshape(block_count, 3, block_len, head_count, head_dim),
        ],
        axis=3,
    )
    grad_pad = jnp.zeros((block_count + 2, block_len, 2, head_count, head_dim), jnp.float32)
    grad_pad = (
        grad_pad.at[:block_count]
        .add(window_terms[:, 0])
        .at[1 : block_count + 1]
        .add(window_terms[:, 1])
        .at[2:]
        .add(window_terms[:, 2])
    )
    global_grad = reduce_to_first(
        jnp.stack([key_first, value_first], axis=1).reshape(block_len, 2 * width_cols), "seq"
    ).reshape(block_len, 2, head_count, head_dim)
    grad_pad = grad_pad.at[1].add(jnp.where(seq_index == 0, global_grad, 0.0))
    rims = jnp.concatenate([grad_pad[0], grad_pad[block_count + 1]], axis=0).reshape(
        2 * block_len, 2 * width_cols
    )
    rim_sums = with_halo(rims.astype(jnp.bfloat16), (("seq", 0),), block_len).astype(rims.dtype)
    core = grad_pad[1 : block_count + 1].reshape(shard_len, 2 * width_cols)
    core = (
        core.at[:block_len]
        .add(rim_sums[:block_len])
        .at[shard_len - block_len :]
        .add(rim_sums[3 * block_len :])
    )
    core = core.reshape(block_count, block_len, 2, head_count, head_dim)
    def give_back(terms):
        terms = terms.reshape(request_count, block_len * head_dim).astype(jnp.bfloat16)
        outgoing = jnp.dot(pick_hot.T, terms, preferred_element_type=jnp.float32).astype(
            jnp.bfloat16
        )
        outgoing = outgoing.reshape(seq_count, capacity, block_len, head_dim)
        incoming = lax.all_to_all(outgoing, "seq", split_axis=0, concat_axis=0, tiled=True)
        return jnp.dot(
            serve_hot.T, incoming.reshape(slot_total, -1), preferred_element_type=jnp.float32
        ).reshape(block_count, head_count, block_len, head_dim)

    added_vals = give_back(value_far)
    added_keys = give_back(key_far)
    added = jnp.stack([added_keys, added_vals], axis=3)
    core = core + jnp.transpose(added, (0, 2, 3, 1, 4))
    grad_k = core[:, :, 0].reshape(shard_len, width_cols).astype(jnp.bfloat16)
    grad_v = core[:, :, 1].reshape(shard_len, width_cols).astype(jnp.bfloat16)
    grad_q_rows = grad_q.reshape(shard_len, width_cols)
    head_index = lax.axis_index("head")

    def to_owners(rows):
        count = rows.shape[0]
        rows = rows.reshape(count, group_count, piece_len, width_cols)
        pieces = [lax.dynamic_index_in_dim(rows, head_index, axis=1, keepdims=False)]
        for shift in range(1, group_count):
            pairs = [(i, (i + shift) % group_count) for i in range(group_count)]
            sent = lax.dynamic_index_in_dim(
                rows, (head_index + shift) % group_count, axis=1, keepdims=False
            )
            pieces.append(lax.ppermute(sent, "head", pairs))
        pieces = jnp.stack(pieces)
        order = (head_index - jnp.arange(group_count, dtype=jnp.int32)) % group_count
        pieces = jnp.take(pieces, order, axis=0)
        return jnp.transpose(pieces, (1, 2, 0, 3)).reshape(
            count, 1, piece_len, group_count * width_cols
        )

    grad_queries = to_owners(grad_q_rows[None])[0]
    back = to_owners(jnp.stack([grad_k, grad_v]))
    grad_keys, grad_values = back[0], back[1]
    return (layer_out, grad_queries, grad_keys, grad_values, weight_grad)


def solution(mesh):
    in_specs = (
        P("dp", ("seq", "head"), None),
        P("dp", ("seq", "head"), None),
        P("dp", ("seq", "head"), None),
        P("seq", "head", None),
        P("head", None),
        P("dp", ("seq", "head"), None),
    )
    out_specs = (
        P("dp", ("seq", "head"), None),
        P("dp", ("seq", "head"), None),
        P("dp", ("seq", "head"), None),
        P("dp", ("seq", "head"), None),
        P("head", None),
    )
    return jax.shard_map(
        per_device, mesh=mesh, in_specs=in_specs, out_specs=out_specs, check_vma=False
    )
```

profile of v0, /device:TPU:1, one launch (start us, length us, event | category | flops | bytes accessed | tf_op | source)
XLA Modules:
  0.0 491.2 jit_solution(13413345749116223735)
XLA Ops:
  14.6 5.3 %reshape.773 = bf16[3,160,4,512]{3,2,1,0:T(4,128)(2,1)} reshape(bf16[3,160,2048]{2,1,0:T(8,128)(2,1)} %pad_maximum_fusion.1) | data formatting | bytes 3932160 | tf_op jit(solution)/shard_map/reshape | solution.py:107
  23.2 4.6 all-to-all-start
  39.4 11.9 %all-to-all-done = bf16[4,3,160,512]{3,2,1,0:T(8,128)(2,1)} async-done(((bf16[4,3,160,512]{3,2,1,0:T(8,128)(2,1)}), bf16[4,3,160,512]{3,2,1,0:T(8,128)(2,1)}, u32[]{:S(2)}, u32[]{:S(2)}) %all-to-all-start) | async-done | bytes 1966112 | tf_op jit(solution)/shard_map/all_to_all | solution.py:108
  76.5 9.1 %all-to-all-start.1 = ((bf16[16,15,64,128]{3,2,1,0:T(8,128)(2,1)}), bf16[16,15,64,128]{3,2,1,0:T(8,128)(2,1)}, u32[]{:S(2)}, u32[]{:S(2)}) async-start(bf16[16,15,64,128]{3,2,1,0:T(8,128)(2,1)} %bitcast.361), calls=%async_computation.1 | async-start | bytes 7864320 | tf_op jit(solution)/shard_map/all_to_all | solution.py:148
  87.6 5.1 %collective-permute-start.2 = (bf16[64,1024]{1,0:T(8,128)(2,1)S(1)}, bf16[64,1024]{1,0:T(8,128)(2,1)}, u32[]{:S(2)}, u32[]{:S(2)}) collective-permute-start(bf16[64,1024]{1,0:T(8,128)(2,1)S(1)} %get-tuple-element.108), channel_id=1, source_target_pairs={{0,48},{1,49},{2,50},{3,51},{64,112},{65,113},{66,114},{67,115}} | collective-permute-start | bytes 393224 | tf_op jit(solution)/shard_map/ppermute | solution.py:37
  102.6 27.2 %collective-permute-done.2 = bf16[64,1024]{1,0:T(8,128)(2,1)} collective-permute-done((bf16[64,1024]{1,0:T(8,128)(2,1)S(1)}, bf16[64,1024]{1,0:T(8,128)(2,1)}, u32[]{:S(2)}, u32[]{:S(2)}) %collective-permute-start.2) | collective-permute-done | bytes 131104 | tf_op jit(solution)/shard_map/ppermute | solution.py:37
  143.2 4.9 %pad_maximum_fusion = bf16[10,3,64,2,4,128]{5,4,3,2,0,1:T(4,128)(2,1)S(1)} fusion(bf16[10,1,64,2,4,128]{5,4,3,2,0,1:T(4,128)(2,1)} %stack.96, bf16[10,1,64,2,4,128]{5,4,3,2,0,1:T(4,128)(2,1)} %stack.95, bf16[10,1,64,2,4,128]{5,4,3,2,0,1:T(4,128)(2,1)} %stack.94), kind=kLoop, calls=%fused_computation.34 | loop fusion | flops 3932160 | bytes 7864320 | tf_op jit(solution)/shard_map/stack | solution.py:157
  155.8 5.8 %all-to-all-start.2 = ((bf16[16,15,64,128]{3,2,1,0:T(8,128)(2,1)}), bf16[16,15,64,128]{3,2,1,0:T(8,128)(2,1)}, u32[]{:S(2)}, u32[]{:S(2)}) async-start(bf16[16,15,64,128]{3,2,1,0:T(8,128)(2,1)} %bitcast.366), calls=%async_computation.2 | async-start | bytes 7864320 | tf_op jit(solution)/shard_map/all_to_all | solution.py:148
  161.6 5.1 %select_reduce_fusion = (f32[4,10,64]{2,1,0:T(8,128)}, f32[4,10,64,192]{3,2,1,0:T(8,128)}) fusion(pred[10,192]{1,0:T(8,128)(4,1)S(1)} %broadcast_in_dim.121, bf16[10,192,2,4,128]{4,1,0,3,2:T(8,128)(2,1)} %bitcast.363, bf16[10,64,4,128]{3,2,1,0:T(4,128)(2,1)S(1)} %reshape_squeeze.2), kind=kOutput, calls=%fused_computation.67 | convolution fusion | flops 127301120 | bytes 4599680 | tf_op jit(solution)/shard_map/ibhd,ikhd->hibk/dot_general | solution.py:172
  176.3 4.8 fusion.52
  191.3 26.5 %all-to-all-done.2 = bf16[16,15,64,128]{3,2,1,0:T(8,128)(2,1)} async-done(((bf16[16,15,64,128]{3,2,1,0:T(8,128)(2,1)}), bf16[16,15,64,128]{3,2,1,0:T(8,128)(2,1)}, u32[]{:S(2)}, u32[]{:S(2)}) %all-to-all-start.2) | async-done | bytes 3932192 | tf_op jit(solution)/shard_map/all_to_all | solution.py:148
  217.8 5.0 %fusion.55 = bf16[20,8,64,128]{3,1,2,0:T(8,128)(2,1)S(1)} fusion(bf16[30,8,64,128]{3,2,1,0:T(8,128)(2,1)} %bitcast.154, s32[160]{0:T(256)S(1)} %convert_add_fusion.1), kind=kOutput, calls=%fused_computation.87 | convolution fusion | flops 630494720 | bytes 6554240 | tf_op jit(solution)/shard_map/dot_general | solution.py:149
  258.0 7.7 %all-to-all-start.4 = ((bf16[16,15,64,128]{3,2,1,0:T(8,128)(2,1)}), bf16[16,15,64,128]{3,2,1,0:T(8,128)(2,1)}, u32[]{:S(2)}, u32[]{:S(2)}) async-start(bf16[16,15,64,128]{3,2,1,0:T(8,128)(2,1)} %bitcast.367), calls=%async_computation.5 | async-start | bytes 7864320 | tf_op jit(solution)/shard_map/all_to_all | solution.py:343
  266.0 5.0 %multiply_convert_fusion.1 = bf16[4,10,64,4,64]{2,4,3,1,0:T(8,128)(2,1)S(1)} fusion(f32[4,10,64,4,64]{2,4,3,1,0:T(8,128)} %copy-done.1, f32[4,10,64]{2,1,0:T(8,128)S(1)} %copy.385, f32[4,10,64]{2,1,0:T(8,128)S(1)} %get-tuple-element.114, bf16[10,4,4,64,128]{4,3,2,1,0:T(8,128)(2,1)} %bitcast.357, bf16[10,64,4,128,1]{3,2,1,0,4:T(4,128)(2,1)S(1)} %bitcast.355), kind=kOutput, calls=%fused_computation.11 | convolution fusion | flops 171048960 | bytes 7229440 | tf_op jit(solution)/shard_map/ibhd,irhtd->hibrt/dot_general | solution.py:255
  290.7 4.7 multiply_convert_fusion.2
  318.9 6.9 %all-to-all-done.4 = bf16[16,15,64,128]{3,2,1,0:T(8,128)(2,1)} async-done(((bf16[16,15,64,128]{3,2,1,0:T(8,128)(2,1)}), bf16[16,15,64,128]{3,2,1,0:T(8,128)(2,1)}, u32[]{:S(2)}, u32[]{:S(2)}) %all-to-all-start.4) | async-done | bytes 3932192 | tf_op jit(solution)/shard_map/all_to_all | solution.py:343
  342.3 39.3 %collective-permute-done.22 = f32[64,1024]{1,0:T(8,128)} collective-permute-done((f32[64,1024]{1,0:T(8,128)}, f32[64,1024]{1,0:T(8,128)}, u32[]{:S(2)}, u32[]{:S(2)}) %collective-permute-start.22) | collective-permute-done | bytes 262176 | tf_op jit(solution)/shard_map/ppermute | solution.py:53
  388.8 4.7 collective-permute-start.23
  411.9 8.9 %all-reduce.3.cloned.1.call-done = bf16[256,2048]{1,0:T(8,128)(2,1)} async-done(((bf16[256,2048]{1,0:T(8,128)(2,1)}), bf16[256,2048]{1,0:T(8,128)(2,1)}) %all-reduce.3.cloned.1.call-update) | async-done | bytes 1048592 | tf_op jit(solution)/shard_map/psum | solution.py:234
  425.6 5.9 %fusion.59 = f32[10,4,64,1,128]{4,0,2,1,3:T(8,128)} fusion(s32[10,4]{0,1:T(4,128)S(1)} %copy-done.36, s32[240]{0:T(256)S(1)} %sub.182, bf16[30,8,64,128]{3,2,1,0:T(8,128)(2,1)} %bitcast.178), kind=kOutput, calls=%fused_computation.94 | convolution fusion | flops 157296000 | bytes 5244000 | tf_op jit(solution)/shard_map/dot_general | solution.py:344
  431.5 5.0 %fusion.58 = f32[10,4,64,1,128]{4,0,2,1,3:T(8,128)S(1)} fusion(s32[10,4]{0,1:T(4,128)S(1)} %copy-done.36, s32[240]{0:T(256)S(1)} %sub.182, bf16[30,8,64,128]{3,2,1,0:T(8,128)(2,1)} %bitcast.169), kind=kOutput, calls=%fused_computation.93 | convolution fusion | flops 157296000 | bytes 5244000 | tf_op jit(solution)/shard_map/dot_general | solution.py:344
  453.9 9.5 %collective-permute-done.27 = bf16[2,160,512]{2,1,0:T(8,128)(2,1)} collective-permute-done((bf16[2,160,512]{2,1,0:T(8,128)(2,1)}, bf16[2,160,512]{2,1,0:T(8,128)(2,1)}, u32[]{:S(2)}, u32[]{:S(2)}) %collective-permute-start.27) | collective-permute-done | bytes 327712 | tf_op jit(solution)/shard_map/ppermute | solution.py:366
  464.7 6.8 %collective-permute-done.25 = bf16[2,160,512]{2,1,0:T(8,128)(2,1)} collective-permute-done((bf16[2,160,512]{2,1,0:T(8,128)(2,1)}, bf16[2,160,512]{2,1,0:T(8,128)(2,1)}, u32[]{:S(2)}, u32[]{:S(2)}) %collective-permute-start.25) | collective-permute-done | bytes 327712 | tf_op jit(solution)/shard_map/ppermute | solution.py:366
  477.9 6.6 %maximum_select_fusion = f32[512,2048]{1,0:T(8,128)} fusion(f32[256,2048]{1,0:T(8,128)} %collective-permute-done.29, f32[256,2048]{1,0:T(8,128)} %convert_multiply_fusion, pred[]{:T(512)S(6)} %eq.179), kind=kLoop, calls=%fused_computation.20 | loop fusion | flops 3145728 | bytes 8388609 | tf_op jit(solution)/shard_map/jit(_where)/select_n | solution.py:238
  (305 shorter events, 249.9 us)
Async XLA Ops:
  23.2 28.1 %all-to-all-start = ((bf16[4,3,160,512]{3,2,1,0:T(8,128)(2,1)}), bf16[4,3,160,512]{3,2,1,0:T(8,128)(2,1)}, u32[]{:S(2)}, u32[]{:S(2)}) async-start(bf16[4,3,160,512]{3,2,1,0:T(8,128)(2,1)} %copy.354), calls=%async_computation | async-start | bytes 3932160 | tf_op jit(solution)/shard_map/all_to_all | solution.py:108
  76.5 79.3 %all-to-all-start.1 = ((bf16[16,15,64,128]{3,2,1,0:T(8,128)(2,1)}), bf16[16,15,64,128]{3,2,1,0:T(8,128)(2,1)}, u32[]{:S(2)}, u32[]{:S(2)}) async-start(bf16[16,15,64,128]{3,2,1,0:T(8,128)(2,1)} %bitcast.361), calls=%async_computation.1 | async-start | bytes 7864320 | tf_op jit(solution)/shard_map/all_to_all | solution.py:148
  85.5 84.7 %all-gather.2.cloned.1.call-start = ((), (), s32[]{:S(2)}) async-start(), calls=%async_computation.7 | async-start | bytes 3276800 | tf_op jit(solution)/shard_map/all_gather | solution.py:223
  87.6 42.2 %collective-permute-start.2 = (bf16[64,1024]{1,0:T(8,128)(2,1)S(1)}, bf16[64,1024]{1,0:T(8,128)(2,1)}, u32[]{:S(2)}, u32[]{:S(2)}) collective-permute-start(bf16[64,1024]{1,0:T(8,128)(2,1)S(1)} %get-tuple-element.108), channel_id=1, source_target_pairs={{0,48},{1,49},{2,50},{3,51},{64,112},{65,113},{66,114},{67,115}} | collective-permute-start | bytes 393224 | tf_op jit(solution)/shard_map/ppermute | solution.py:37
  92.7 37.1 %collective-permute-start.3 = (bf16[64,1024]{1,0:T(8,128)(2,1)S(1)}, bf16[64,1024]{1,0:T(8,128)(2,1)}, u32[]{:S(2)}, u32[]{:S(2)}) collective-permute-start(bf16[64,1024]{1,0:T(8,128)(2,1)S(1)} %get-tuple-element.108), channel_id=1, source_target_pairs={{0,32},{1,33},{2,34},{3,35},{64,96},{65,97},{66,98},{67,99}} | collective-permute-start | bytes 393224 | tf_op jit(solution)/shard_map/ppermute | solution.py:37
  94.6 35.2 %collective-permute-start.4 = (bf16[64,1024]{1,0:T(8,128)(2,1)S(1)}, bf16[64,1024]{1,0:T(8,128)(2,1)}, u32[]{:S(2)}, u32[]{:S(2)}) collective-permute-start(bf16[64,1024]{1,0:T(8,128)(2,1)S(1)} %get-tuple-element.108), channel_id=1, source_target_pairs={{0,16},{1,17},{2,18},{3,19},{64,80},{65,81},{66,82},{67,83}} | collective-permute-start | bytes 393224 | tf_op jit(solution)/shard_map/ppermute | solution.py:37
  130.5 36.2 %collective-permute-start.5 = (bf16[64,1024]{1,0:T(8,128)(2,1)}, bf16[64,1024]{1,0:T(8,128)(2,1)S(1)}, u32[]{:S(2)}, u32[]{:S(2)}) collective-permute-start(bf16[64,1024]{1,0:T(8,128)(2,1)} %select_select_fusion.1), channel_id=1, source_target_pairs={{0,12},{16,28},{32,44},{48,60},{1,13},{17,29},{33,45},{49,61},{2,1... | collective-permute-start | bytes 393224 | tf_op jit(solution)/shard_map/ppermute | solution.py:37
  131.8 34.9 %collective-permute-start.6 = (bf16[64,1024]{1,0:T(8,128)(2,1)}, bf16[64,1024]{1,0:T(8,128)(2,1)}, u32[]{:S(2)}, u32[]{:S(2)}) collective-permute-start(bf16[64,1024]{1,0:T(8,128)(2,1)} %select_select_fusion.1), channel_id=1, source_target_pairs={{0,8},{16,24},{32,40},{48,56},{1,9},{17,25},{33,41},{49,57},{2,10}... | collective-permute-start | bytes 393224 | tf_op jit(solution)/shard_map/ppermute | solution.py:37
  133.8 33.0 %collective-permute-start.7 = (bf16[64,1024]{1,0:T(8,128)(2,1)}, bf16[64,1024]{1,0:T(8,128)(2,1)}, u32[]{:S(2)}, u32[]{:S(2)}) collective-permute-start(bf16[64,1024]{1,0:T(8,128)(2,1)} %select_select_fusion.1), channel_id=1, source_target_pairs={{0,4},{16,20},{32,36},{48,52},{1,5},{17,21},{33,37},{49,53},{2,6},... | collective-permute-start | bytes 393224 | tf_op jit(solution)/shard_map/ppermute | solution.py:37
  155.8 62.0 %all-to-all-start.2 = ((bf16[16,15,64,128]{3,2,1,0:T(8,128)(2,1)}), bf16[16,15,64,128]{3,2,1,0:T(8,128)(2,1)}, u32[]{:S(2)}, u32[]{:S(2)}) async-start(bf16[16,15,64,128]{3,2,1,0:T(8,128)(2,1)} %bitcast.366), calls=%async_computation.2 | async-start | bytes 7864320 | tf_op jit(solution)/shard_map/all_to_all | solution.py:148
  236.2 98.3 %collective-permute-start.19 = (f32[64,1024]{1,0:T(8,128)}, f32[64,1024]{1,0:T(8,128)}, u32[]{:S(2)}, u32[]{:S(2)}) collective-permute-start(f32[64,1024]{1,0:T(8,128)} %reshape.787), channel_id=1, source_target_pairs={{12,0},{28,16},{44,32},{60,48},{13,1},{29,17},{45,33},{61,49},{14,... | collective-permute-start | bytes 786440 | tf_op jit(solution)/shard_map/ppermute | solution.py:53
  237.5 97.0 %collective-permute-start.18 = (f32[64,1024]{1,0:T(8,128)}, f32[64,1024]{1,0:T(8,128)}, u32[]{:S(2)}, u32[]{:S(2)}) collective-permute-start(f32[64,1024]{1,0:T(8,128)} %reshape.787), channel_id=1, source_target_pairs={{8,0},{24,16},{40,32},{56,48},{9,1},{25,17},{41,33},{57,49},{10,2}... | collective-permute-start | bytes 786440 | tf_op jit(solution)/shard_map/ppermute | solution.py:53
  238.8 95.7 %collective-permute-start.17 = (f32[64,1024]{1,0:T(8,128)}, f32[64,1024]{1,0:T(8,128)}, u32[]{:S(2)}, u32[]{:S(2)}) collective-permute-start(f32[64,1024]{1,0:T(8,128)} %reshape.787), channel_id=1, source_target_pairs={{4,0},{20,16},{36,32},{52,48},{5,1},{21,17},{37,33},{53,49},{6,2},... | collective-permute-start | bytes 786440 | tf_op jit(solution)/shard_map/ppermute | solution.py:53
  258.0 67.8 %all-to-all-start.4 = ((bf16[16,15,64,128]{3,2,1,0:T(8,128)(2,1)}), bf16[16,15,64,128]{3,2,1,0:T(8,128)(2,1)}, u32[]{:S(2)}, u32[]{:S(2)}) async-start(bf16[16,15,64,128]{3,2,1,0:T(8,128)(2,1)} %bitcast.367), calls=%async_computation.5 | async-start | bytes 7864320 | tf_op jit(solution)/shard_map/all_to_all | solution.py:343
  265.7 155.0 %all-reduce.3.cloned.1.call-start = ((), (), s32[]{:S(2)}) async-start(), calls=%async_computation.8 | async-start | bytes 2097152 | tf_op jit(solution)/shard_map/psum | solution.py:234
  278.6 205.9 %reduce-scatter.2.cloned.1.call-start = ((), (), s32[]{:S(2)}) async-start(), calls=%async_computation.6 | async-start | bytes 3276800 | tf_op jit(solution)/shard_map/reduce_scatter | solution.py:217
  325.8 105.7 %all-to-all-start.3 = ((bf16[16,15,64,128]{3,2,1,0:T(8,128)(2,1)}), bf16[16,15,64,128]{3,2,1,0:T(8,128)(2,1)}, u32[]{:S(2)}, u32[]{:S(2)}) async-start(bf16[16,15,64,128]{3,2,1,0:T(8,128)(2,1)} %bitcast.365), calls=%async_computation.4 | async-start | bytes 7864320 | tf_op jit(solution)/shard_map/all_to_all | solution.py:343
  336.6 45.0 %collective-permute-start.22 = (f32[64,1024]{1,0:T(8,128)}, f32[64,1024]{1,0:T(8,128)}, u32[]{:S(2)}, u32[]{:S(2)}) collective-permute-start(f32[64,1024]{1,0:T(8,128)} %add_add_fusion), channel_id=1, source_target_pairs={{48,0},{49,1},{50,2},{51,3},{112,64},{113,65},{114,66},{115,67}} | collective-permute-start | bytes 786440 | tf_op jit(solution)/shard_map/ppermute | solution.py:53
  337.9 43.7 %collective-permute-start.21 = (f32[64,1024]{1,0:T(8,128)}, f32[64,1024]{1,0:T(8,128)}, u32[]{:S(2)}, u32[]{:S(2)}) collective-permute-start(f32[64,1024]{1,0:T(8,128)} %add_add_fusion), channel_id=1, source_target_pairs={{32,0},{33,1},{34,2},{35,3},{96,64},{97,65},{98,66},{99,67}} | collective-permute-start | bytes 786440 | tf_op jit(solution)/shard_map/ppermute | solution.py:53
  339.2 42.4 %collective-permute-start.20 = (f32[64,1024]{1,0:T(8,128)}, f32[64,1024]{1,0:T(8,128)}, u32[]{:S(2)}, u32[]{:S(2)}) collective-permute-start(f32[64,1024]{1,0:T(8,128)} %add_add_fusion), channel_id=1, source_target_pairs={{16,0},{17,1},{18,2},{19,3},{80,64},{81,65},{82,66},{83,67}} | collective-permute-start | bytes 786440 | tf_op jit(solution)/shard_map/ppermute | solution.py:53
  394.3 55.7 %collective-permute-start.16 = (bf16[1,160,512]{2,1,0:T(8,128)(2,1)}, bf16[1,160,512]{2,1,0:T(8,128)(2,1)}, u32[]{:S(2)}, u32[]{:S(2)}) collective-permute-start(bf16[1,160,512]{2,1,0:T(8,128)(2,1)} %get-tuple-element.110), channel_id=1, source_target_pairs={{0,3},{1,0},{2,1},{3,2},{4,7},{5,4},{6,5},{7,6},{8,11},{9,8},{10,9... | collective-permute-start | bytes 491528 | tf_op jit(solution)/shard_map/ppermute | solution.py:366
  395.2 55.2 %collective-permute-start.15 = (bf16[1,160,512]{2,1,0:T(8,128)(2,1)}, bf16[1,160,512]{2,1,0:T(8,128)(2,1)}, u32[]{:S(2)}, u32[]{:S(2)}) collective-permute-start(bf16[1,160,512]{2,1,0:T(8,128)(2,1)} %get-tuple-element.111), channel_id=1, source_target_pairs={{0,2},{1,3},{2,0},{3,1},{4,6},{5,7},{6,4},{7,5},{8,10},{9,11},{10,... | collective-permute-start | bytes 491528 | tf_op jit(solution)/shard_map/ppermute | solution.py:366
  396.3 54.7 %collective-permute-start.14 = (bf16[1,160,512]{2,1,0:T(8,128)(2,1)}, bf16[1,160,512]{2,1,0:T(8,128)(2,1)}, u32[]{:S(2)}, u32[]{:S(2)}) collective-permute-start(bf16[1,160,512]{2,1,0:T(8,128)(2,1)} %get-tuple-element.109), channel_id=1, source_target_pairs={{0,1},{1,2},{2,3},{3,0},{4,5},{5,6},{6,7},{7,4},{8,9},{9,10},{10,1... | collective-permute-start | bytes 491528 | tf_op jit(solution)/shard_map/ppermute | solution.py:366
  423.5 54.4 %collective-permute-start.29 = (f32[256,2048]{1,0:T(8,128)}, f32[256,2048]{1,0:T(8,128)}, u32[]{:S(2)}, u32[]{:S(2)}) collective-permute-start(f32[256,2048]{1,0:T(8,128)} %convert_multiply_fusion), channel_id=1, source_target_pairs={{0,64},{64,0},{1,65},{65,1},{2,66},{66,2},{3,67},{67,3},{4,68},{68... | collective-permute-start | bytes 6291464 | tf_op jit(solution)/shard_map/ppermute | solution.py:237
  (53 other events, 505.8 us)
Sparse Core Ops, SparseCore 0:
  88.0 38.0 all-gather.1
  278.7 141.9 all-reduce.2
  423.7 43.9 reduce-scatter.1
where the time goes:
time: 501 us; the launch traced here: 491 us
  waiting for transfers between devices  146 us (29%)
  local copies, waits for them, and re-layouts  108 us (22%)
  starting transfers between devices  84.3 us (17%)
  matrix products  71.4 us (14%)
  other arithmetic  65.7 us (13%)
  between operations  15.1 us (3%)
    ppermute x6, waiting for transfers between devices, reduce_to_first(): total = total + lax.ppermute(block, axis, pairs)  39.3 us
    unnamed x87, local copies, waits for them, and re-layouts  27.7 us
    ppermute x6, waiting for transfers between devices, broadcast_first(): got = lax.ppermute(block, axis, pairs)  27.2 us
    all_to_all x2, waiting for transfers between devices, fetch(): lax.all_to_all(served, 'seq', split_axis=0, concat_axis=0, tiled=True)  26.6 us
    ppermute x6, waiting for transfers between devices, to_owners(): pieces.append(lax.ppermute(sent, 'head', pairs))  17.6 us
    all_to_all x2, starting transfers between devices, fetch(): lax.all_to_all(served, 'seq', split_axis=0, concat_axis=0, tiled=True)  14.9 us
    ppermute x6, starting transfers between devices, broadcast_first(): got = lax.ppermute(block, axis, pairs)  14.3 us
    another operation x4, local copies, waits for them, and re-layouts, per_device(): jnp.stack([pair_view[:block_count], pair_view[1:block_count + 1], pair_vi...  12.4 us
  transfers between devices with their start and end apart: 38, of which 14 were waited for; matrix products, arithmetic and copies ran while one was open for 42% of the time, Pallas kernels for 0%

commit v1 on v0

--- a/solution.py
+++ b/solution.py
@@ -50,7 +50,8 @@
         for m in range(1, radix):
             pairs = [(j + m * stride, j) for j in range(0, count, span) if j + m * stride < count]
             if pairs:
-                total = total + lax.ppermute(block, axis, pairs)
+                sent = lax.ppermute(block.astype(jnp.bfloat16), axis, pairs)
+                total = total + sent.astype(block.dtype)
         block = total
         stride *= radix
     return block
@@ -231,14 +232,12 @@
     mine = lax.dynamic_slice_in_dim(weight_acc, dp_index * half_rows, half_rows, axis=0)
     theirs = lax.dynamic_slice_in_dim(weight_acc, (1 - dp_index) * half_rows, half_rows, axis=0)
     mine = mine + lax.ppermute(theirs, "dp", [(0, 1), (1, 0)])
-    mine = lax.psum(mine.astype(jnp.bfloat16), "seq").astype(jnp.float32) * (
+    mine = lax.psum(mine.astype(jnp.bfloat16), "seq")
+    other = lax.ppermute(mine, "dp", [(0, 1), (1, 0)])
+    low = jnp.where(dp_index == 0, mine, other)
+    high = jnp.where(dp_index == 0, other, mine)
+    weight_grad = jnp.concatenate([low, high], axis=0).astype(jnp.float32) * (
         1.0 / math.sqrt(token_total)
-    )
-    other = lax.ppermute(mine, "dp", [(0, 1), (1, 0)])
-    weight_grad = jnp.where(
-        dp_index == 0,
-        jnp.concatenate([mine, other], axis=0),
-        jnp.concatenate([other, mine], axis=0),
     )
     grad_blocks = grad_piece.reshape(block_count, block_len, head_count, head_dim)
     delta_rows = jnp.sum(grad_blocks.astype(jnp.float32) * attn.astype(jnp.float32), axis=-1)

time: 501 us -> 517 us (1.032)
  waiting for transfers between devices: 146 us -> 162 us
  local copies, waits for them, and re-layouts: 108 us -> 115 us
    psum x1, waiting for transfers between devices: 8.89 us -> 35.8 us  [per_device(): mine = lax.psum(mine.astype(jnp.bfloat16), 'seq')]
    ppermute x6, waiting for transfers between devices: 39.3 us -> 25.5 us  [reduce_to_first(): sent = lax.ppermute(block.astype(jnp.bfloat16), axis, pairs)]
    select_n x1, other arithmetic: 6.56 us -> 1.37 us  [per_device(): low = jnp.where(dp_index == 0, mine, other)]
    unnamed x87 -> x93, local copies, waits for them, and re-layouts: 27.7 us -> 31.7 us
  transfers between devices with their start and end apart: 38 -> 38, of which waited for: 14 -> 14; matrix products, arithmetic and copies ran while one was open for 42% -> 39% of each run, Pallas kernels for 0% -> 0%
where the time goes in v1:
time: 517 us; the launch traced here: 507 us
  waiting for transfers between devices  162 us (31%)
  local copies, waits for them, and re-layouts  115 us (22%)
  starting transfers between devices  85.8 us (17%)
  matrix products  68.7 us (13%)
  other arithmetic  61.3 us (12%)
  between operations  15.2 us (3%)
    psum x1, waiting for transfers between devices, per_device(): mine = lax.psum(mine.astype(jnp.bfloat16), 'seq')  35.8 us
    unnamed x93, local copies, waits for them, and re-layouts  31.7 us
    ppermute x6, waiting for transfers between devices, broadcast_first(): got = lax.ppermute(block, axis, pairs)  27.2 us
    all_to_all x2, waiting for transfers between devices, fetch(): lax.all_to_all(served, 'seq', split_axis=0, concat_axis=0, tiled=True)  26.5 us
    ppermute x6, waiting for transfers between devices, reduce_to_first(): sent = lax.ppermute(block.astype(jnp.bfloat16), axis, pairs)  25.5 us
    ppermute x6, waiting for transfers between devices, to_owners(): pieces.append(lax.ppermute(sent, 'head', pairs))  20.4 us
    all_to_all x2, starting transfers between devices, fetch(): lax.all_to_all(served, 'seq', split_axis=0, concat_axis=0, tiled=True)  14.9 us
    ppermute x6, starting transfers between devices, broadcast_first(): got = lax.ppermute(block, axis, pairs)  14.3 us
  transfers between devices with their start and end apart: 38, of which 14 were waited for; matrix products, arithmetic and copies ran while one was open for 39% of the time, Pallas kernels for 0%

profile of v1, /device:TPU:1, one launch (start us, length us, event | category | flops | bytes accessed | tf_op | source)
XLA Modules:
  0.0 507.5 jit_solution(9634821017772570473)
XLA Ops:
  14.6 5.3 %reshape.773 = bf16[3,160,4,512]{3,2,1,0:T(4,128)(2,1)} reshape(bf16[3,160,2048]{2,1,0:T(8,128)(2,1)} %pad_maximum_fusion.1) | data formatting | bytes 3932160 | tf_op jit(solution)/shard_map/reshape | solution.py:108
  39.4 11.8 %all-to-all-done = bf16[4,3,160,512]{3,2,1,0:T(8,128)(2,1)} async-done(((bf16[4,3,160,512]{3,2,1,0:T(8,128)(2,1)}), bf16[4,3,160,512]{3,2,1,0:T(8,128)(2,1)}, u32[]{:S(2)}, u32[]{:S(2)}) %all-to-all-start) | async-done | bytes 1966112 | tf_op jit(solution)/shard_map/all_to_all | solution.py:109
  64.3 4.9 pad_maximum_fusion.5
  77.0 9.1 %all-to-all-start.1 = ((bf16[16,15,64,128]{3,2,1,0:T(8,128)(2,1)}), bf16[16,15,64,128]{3,2,1,0:T(8,128)(2,1)}, u32[]{:S(2)}, u32[]{:S(2)}) async-start(bf16[16,15,64,128]{3,2,1,0:T(8,128)(2,1)} %bitcast.361), calls=%async_computation.1 | async-start | bytes 7864320 | tf_op jit(solution)/shard_map/all_to_all | solution.py:149
  88.1 5.1 %collective-permute-start.2 = (bf16[64,1024]{1,0:T(8,128)(2,1)S(1)}, bf16[64,1024]{1,0:T(8,128)(2,1)}, u32[]{:S(2)}, u32[]{:S(2)}) collective-permute-start(bf16[64,1024]{1,0:T(8,128)(2,1)S(1)} %get-tuple-element.110), channel_id=1, source_target_pairs={{0,48},{1,49},{2,50},{3,51},{64,112},{65,113},{66,114},{67,115}} | collective-permute-start | bytes 393224 | tf_op jit(solution)/shard_map/ppermute | solution.py:37
  103.1 27.2 %collective-permute-done.2 = bf16[64,1024]{1,0:T(8,128)(2,1)} collective-permute-done((bf16[64,1024]{1,0:T(8,128)(2,1)S(1)}, bf16[64,1024]{1,0:T(8,128)(2,1)}, u32[]{:S(2)}, u32[]{:S(2)}) %collective-permute-start.2) | collective-permute-done | bytes 131104 | tf_op jit(solution)/shard_map/ppermute | solution.py:37
  143.7 4.9 pad_maximum_fusion
  156.1 5.8 %all-to-all-start.2 = ((bf16[16,15,64,128]{3,2,1,0:T(8,128)(2,1)}), bf16[16,15,64,128]{3,2,1,0:T(8,128)(2,1)}, u32[]{:S(2)}, u32[]{:S(2)}) async-start(bf16[16,15,64,128]{3,2,1,0:T(8,128)(2,1)} %bitcast.366), calls=%async_computation.2 | async-start | bytes 7864320 | tf_op jit(solution)/shard_map/all_to_all | solution.py:149
  162.0 5.0 select_reduce_fusion
  176.8 4.8 fusion.52
  191.7 26.5 %all-to-all-done.2 = bf16[16,15,64,128]{3,2,1,0:T(8,128)(2,1)} async-done(((bf16[16,15,64,128]{3,2,1,0:T(8,128)(2,1)}), bf16[16,15,64,128]{3,2,1,0:T(8,128)(2,1)}, u32[]{:S(2)}, u32[]{:S(2)}) %all-to-all-start.2) | async-done | bytes 3932192 | tf_op jit(solution)/shard_map/all_to_all | solution.py:149
  218.2 5.0 fusion.55
  244.5 6.6 %multiply_convert_fusion.1 = bf16[4,10,64,4,64]{2,4,3,1,0:T(8,128)(2,1)} fusion(f32[4,10,64,4,64]{2,4,3,1,0:T(8,128)} %copy-done.1, f32[4,10,64]{2,1,0:T(8,128)S(1)} %copy.385, f32[4,10,64]{2,1,0:T(8,128)S(1)} %get-tuple-element.116, bf16[10,4,4,64,128]{4,3,2,1,0:T(8,128)(2,1)} %bitcast.357, bf16[10,64,4,128,1]{3,2,1,0,4:T(4,128)(2,1)S(1)} %bitcast.355), kind=kOutput, calls=%fused_computation.11 | convolution fusion | flops 171048960 | bytes 7229440 | tf_op jit(solution)/shard_map/ibhd,irhtd->hibrt/dot_general | solution.py:254
  258.9 7.3 %all-to-all-start.4 = ((bf16[16,15,64,128]{3,2,1,0:T(8,128)(2,1)}), bf16[16,15,64,128]{3,2,1,0:T(8,128)(2,1)}, u32[]{:S(2)}, u32[]{:S(2)}) async-start(bf16[16,15,64,128]{3,2,1,0:T(8,128)(2,1)} %bitcast.367), calls=%async_computation.5 | async-start | bytes 7864320 | tf_op jit(solution)/shard_map/all_to_all | solution.py:342
  310.8 6.6 %all-to-all-done.4 = bf16[16,15,64,128]{3,2,1,0:T(8,128)(2,1)} async-done(((bf16[16,15,64,128]{3,2,1,0:T(8,128)(2,1)}), bf16[16,15,64,128]{3,2,1,0:T(8,128)(2,1)}, u32[]{:S(2)}, u32[]{:S(2)}) %all-to-all-start.4) | async-done | bytes 3932192 | tf_op jit(solution)/shard_map/all_to_all | solution.py:342
  317.4 6.1 %all-to-all-start.3 = ((bf16[16,15,64,128]{3,2,1,0:T(8,128)(2,1)}), bf16[16,15,64,128]{3,2,1,0:T(8,128)(2,1)}, u32[]{:S(2)}, u32[]{:S(2)}) async-start(bf16[16,15,64,128]{3,2,1,0:T(8,128)(2,1)} %bitcast.362), calls=%async_computation.4 | async-start | bytes 7864320 | tf_op jit(solution)/shard_map/all_to_all | solution.py:342
  330.3 4.8 fusion.19
  348.4 25.5 %collective-permute-done.22 = bf16[64,1024]{1,0:T(8,128)(2,1)S(1)} collective-permute-done((bf16[64,1024]{1,0:T(8,128)(2,1)}, bf16[64,1024]{1,0:T(8,128)(2,1)S(1)}, u32[]{:S(2)}, u32[]{:S(2)}) %collective-permute-start.22) | collective-permute-done | bytes 131104 | tf_op jit(solution)/shard_map/ppermute | solution.py:53
  381.1 4.6 collective-permute-start.23
  403.8 35.8 %all-reduce.3.cloned.1.call-done = bf16[256,2048]{1,0:T(8,128)(2,1)} async-done(((bf16[256,2048]{1,0:T(8,128)(2,1)}), bf16[256,2048]{1,0:T(8,128)(2,1)}) %all-reduce.3.cloned.1.call-update) | async-done | bytes 1048592 | tf_op jit(solution)/shard_map/psum | solution.py:235
  441.8 5.9 %fusion.59 = f32[10,4,64,1,128]{4,0,2,1,3:T(8,128)} fusion(s32[10,4]{0,1:T(4,128)S(1)} %copy-done.39, s32[240]{0:T(256)S(1)} %sub.182, bf16[30,8,64,128]{3,2,1,0:T(8,128)(2,1)} %bitcast.178), kind=kOutput, calls=%fused_computation.93 | convolution fusion | flops 157296000 | bytes 5244000 | tf_op jit(solution)/shard_map/dot_general | solution.py:343
  447.7 4.7 fusion.58
  469.9 10.5 %collective-permute-done.27 = bf16[2,160,512]{2,1,0:T(8,128)(2,1)} collective-permute-done((bf16[2,160,512]{2,1,0:T(8,128)(2,1)}, bf16[2,160,512]{2,1,0:T(8,128)(2,1)}, u32[]{:S(2)}, u32[]{:S(2)}) %collective-permute-start.27) | collective-permute-done | bytes 327712 | tf_op jit(solution)/shard_map/ppermute | solution.py:365
  483.5 6.8 %collective-permute-done.25 = bf16[2,160,512]{2,1,0:T(8,128)(2,1)} collective-permute-done((bf16[2,160,512]{2,1,0:T(8,128)(2,1)}, bf16[2,160,512]{2,1,0:T(8,128)(2,1)}, u32[]{:S(2)}, u32[]{:S(2)}) %collective-permute-start.25) | collective-permute-done | bytes 327712 | tf_op jit(solution)/shard_map/ppermute | solution.py:365
  (312 shorter events, 251.8 us)
Async XLA Ops:
  77.0 79.2 %all-to-all-start.1 = ((bf16[16,15,64,128]{3,2,1,0:T(8,128)(2,1)}), bf16[16,15,64,128]{3,2,1,0:T(8,128)(2,1)}, u32[]{:S(2)}, u32[]{:S(2)}) async-start(bf16[16,15,64,128]{3,2,1,0:T(8,128)(2,1)} %bitcast.361), calls=%async_computation.1 | async-start | bytes 7864320 | tf_op jit(solution)/shard_map/all_to_all | solution.py:149
  86.0 84.6 %all-gather.2.cloned.1.call-start = ((), (), s32[]{:S(2)}) async-start(), calls=%async_computation.7 | async-start | bytes 3276800 | tf_op jit(solution)/shard_map/all_gather | solution.py:224
  88.1 42.2 %collective-permute-start.2 = (bf16[64,1024]{1,0:T(8,128)(2,1)S(1)}, bf16[64,1024]{1,0:T(8,128)(2,1)}, u32[]{:S(2)}, u32[]{:S(2)}) collective-permute-start(bf16[64,1024]{1,0:T(8,128)(2,1)S(1)} %get-tuple-element.110), channel_id=1, source_target_pairs={{0,48},{1,49},{2,50},{3,51},{64,112},{65,113},{66,114},{67,115}} | collective-permute-start | bytes 393224 | tf_op jit(solution)/shard_map/ppermute | solution.py:37
  93.2 37.1 %collective-permute-start.3 = (bf16[64,1024]{1,0:T(8,128)(2,1)S(1)}, bf16[64,1024]{1,0:T(8,128)(2,1)}, u32[]{:S(2)}, u32[]{:S(2)}) collective-permute-start(bf16[64,1024]{1,0:T(8,128)(2,1)S(1)} %get-tuple-element.110), channel_id=1, source_target_pairs={{0,32},{1,33},{2,34},{3,35},{64,96},{65,97},{66,98},{67,99}} | collective-permute-start | bytes 393224 | tf_op jit(solution)/shard_map/ppermute | solution.py:37
  95.2 35.1 %collective-permute-start.4 = (bf16[64,1024]{1,0:T(8,128)(2,1)S(1)}, bf16[64,1024]{1,0:T(8,128)(2,1)}, u32[]{:S(2)}, u32[]{:S(2)}) collective-permute-start(bf16[64,1024]{1,0:T(8,128)(2,1)S(1)} %get-tuple-element.110), channel_id=1, source_target_pairs={{0,16},{1,17},{2,18},{3,19},{64,80},{65,81},{66,82},{67,83}} | collective-permute-start | bytes 393224 | tf_op jit(solution)/shard_map/ppermute | solution.py:37
  131.0 36.0 %collective-permute-start.5 = (bf16[64,1024]{1,0:T(8,128)(2,1)}, bf16[64,1024]{1,0:T(8,128)(2,1)S(1)}, u32[]{:S(2)}, u32[]{:S(2)}) collective-permute-start(bf16[64,1024]{1,0:T(8,128)(2,1)} %select_select_fusion.1), channel_id=1, source_target_pairs={{0,12},{16,28},{32,44},{48,60},{1,13},{17,29},{33,45},{49,61},{2,1... | collective-permute-start | bytes 393224 | tf_op jit(solution)/shard_map/ppermute | solution.py:37
  132.3 34.7 %collective-permute-start.6 = (bf16[64,1024]{1,0:T(8,128)(2,1)}, bf16[64,1024]{1,0:T(8,128)(2,1)}, u32[]{:S(2)}, u32[]{:S(2)}) collective-permute-start(bf16[64,1024]{1,0:T(8,128)(2,1)} %select_select_fusion.1), channel_id=1, source_target_pairs={{0,8},{16,24},{32,40},{48,56},{1,9},{17,25},{33,41},{49,57},{2,10}... | collective-permute-start | bytes 393224 | tf_op jit(solution)/shard_map/ppermute | solution.py:37
  134.3 32.7 %collective-permute-start.7 = (bf16[64,1024]{1,0:T(8,128)(2,1)}, bf16[64,1024]{1,0:T(8,128)(2,1)}, u32[]{:S(2)}, u32[]{:S(2)}) collective-permute-start(bf16[64,1024]{1,0:T(8,128)(2,1)} %select_select_fusion.1), channel_id=1, source_target_pairs={{0,4},{16,20},{32,36},{48,52},{1,5},{17,21},{33,37},{49,53},{2,6},... | collective-permute-start | bytes 393224 | tf_op jit(solution)/shard_map/ppermute | solution.py:37
  156.1 62.0 %all-to-all-start.2 = ((bf16[16,15,64,128]{3,2,1,0:T(8,128)(2,1)}), bf16[16,15,64,128]{3,2,1,0:T(8,128)(2,1)}, u32[]{:S(2)}, u32[]{:S(2)}) async-start(bf16[16,15,64,128]{3,2,1,0:T(8,128)(2,1)} %bitcast.366), calls=%async_computation.2 | async-start | bytes 7864320 | tf_op jit(solution)/shard_map/all_to_all | solution.py:149
  238.2 98.4 %collective-permute-start.19 = (bf16[64,1024]{1,0:T(8,128)(2,1)}, bf16[64,1024]{1,0:T(8,128)(2,1)}, u32[]{:S(2)}, u32[]{:S(2)}) collective-permute-start(bf16[64,1024]{1,0:T(8,128)(2,1)} %convert_element_type.197), channel_id=1, source_target_pairs={{12,0},{28,16},{44,32},{60,48},{13,1},{29,17},{45,33},{61,49},{14,... | collective-permute-start | bytes 393224 | tf_op jit(solution)/shard_map/ppermute | solution.py:53
  239.5 97.1 %collective-permute-start.18 = (bf16[64,1024]{1,0:T(8,128)(2,1)}, bf16[64,1024]{1,0:T(8,128)(2,1)}, u32[]{:S(2)}, u32[]{:S(2)}) collective-permute-start(bf16[64,1024]{1,0:T(8,128)(2,1)} %convert_element_type.197), channel_id=1, source_target_pairs={{8,0},{24,16},{40,32},{56,48},{9,1},{25,17},{41,33},{57,49},{10,2}... | collective-permute-start | bytes 393224 | tf_op jit(solution)/shard_map/ppermute | solution.py:53
  240.8 95.8 %collective-permute-start.17 = (bf16[64,1024]{1,0:T(8,128)(2,1)}, bf16[64,1024]{1,0:T(8,128)(2,1)}, u32[]{:S(2)}, u32[]{:S(2)}) collective-permute-start(bf16[64,1024]{1,0:T(8,128)(2,1)} %convert_element_type.197), channel_id=1, source_target_pairs={{4,0},{20,16},{36,32},{52,48},{5,1},{21,17},{37,33},{53,49},{6,2},... | collective-permute-start | bytes 393224 | tf_op jit(solution)/shard_map/ppermute | solution.py:53
  258.9 58.5 %all-to-all-start.4 = ((bf16[16,15,64,128]{3,2,1,0:T(8,128)(2,1)}), bf16[16,15,64,128]{3,2,1,0:T(8,128)(2,1)}, u32[]{:S(2)}, u32[]{:S(2)}) async-start(bf16[16,15,64,128]{3,2,1,0:T(8,128)(2,1)} %bitcast.367), calls=%async_computation.5 | async-start | bytes 7864320 | tf_op jit(solution)/shard_map/all_to_all | solution.py:342
  277.5 46.1 %collective-permute-start.28 = (f32[256,2048]{1,0:T(8,128)}, f32[256,2048]{1,0:T(8,128)}, u32[]{:S(2)}, u32[]{:S(2)}) collective-permute-start(f32[256,2048]{1,0:T(8,128)} %constant_dynamic-slice_fusion), channel_id=1, source_target_pairs={{0,64},{64,0},{1,65},{65,1},{2,66},{66,2},{3,67},{67,3},{4,68},{68... | collective-permute-start | bytes 6291464 | tf_op jit(solution)/shard_map/ppermute | solution.py:234
  317.4 130.3 %all-to-all-start.3 = ((bf16[16,15,64,128]{3,2,1,0:T(8,128)(2,1)}), bf16[16,15,64,128]{3,2,1,0:T(8,128)(2,1)}, u32[]{:S(2)}, u32[]{:S(2)}) async-start(bf16[16,15,64,128]{3,2,1,0:T(8,128)(2,1)} %bitcast.362), calls=%async_computation.4 | async-start | bytes 7864320 | tf_op jit(solution)/shard_map/all_to_all | solution.py:342
  323.5 116.1 %all-reduce.3.cloned.1.call-start = ((), (), s32[]{:S(2)}) async-start(), calls=%async_computation.8 | async-start | bytes 2097152 | tf_op jit(solution)/shard_map/psum | solution.py:235
  327.1 173.6 %reduce-scatter.2.cloned.1.call-start = ((), (), s32[]{:S(2)}) async-start(), calls=%async_computation.6 | async-start | bytes 3276800 | tf_op jit(solution)/shard_map/reduce_scatter | solution.py:218
  338.4 35.4 %collective-permute-start.22 = (bf16[64,1024]{1,0:T(8,128)(2,1)}, bf16[64,1024]{1,0:T(8,128)(2,1)S(1)}, u32[]{:S(2)}, u32[]{:S(2)}) collective-permute-start(bf16[64,1024]{1,0:T(8,128)(2,1)} %fusion.170), channel_id=1, source_target_pairs={{48,0},{49,1},{50,2},{51,3},{112,64},{113,65},{114,66},{115,67}} | collective-permute-start | bytes 393224 | tf_op jit(solution)/shard_map/ppermute | solution.py:53
  339.7 34.2 %collective-permute-start.21 = (bf16[64,1024]{1,0:T(8,128)(2,1)}, bf16[64,1024]{1,0:T(8,128)(2,1)}, u32[]{:S(2)}, u32[]{:S(2)}) collective-permute-start(bf16[64,1024]{1,0:T(8,128)(2,1)} %fusion.170), channel_id=1, source_target_pairs={{32,0},{33,1},{34,2},{35,3},{96,64},{97,65},{98,66},{99,67}} | collective-permute-start | bytes 393224 | tf_op jit(solution)/shard_map/ppermute | solution.py:53
  341.0 32.9 %collective-permute-start.20 = (bf16[64,1024]{1,0:T(8,128)(2,1)}, bf16[64,1024]{1,0:T(8,128)(2,1)}, u32[]{:S(2)}, u32[]{:S(2)}) collective-permute-start(bf16[64,1024]{1,0:T(8,128)(2,1)} %fusion.170), channel_id=1, source_target_pairs={{16,0},{17,1},{18,2},{19,3},{80,64},{81,65},{82,66},{83,67}} | collective-permute-start | bytes 393224 | tf_op jit(solution)/shard_map/ppermute | solution.py:53
  386.5 79.4 %collective-permute-start.16 = (bf16[1,160,512]{2,1,0:T(8,128)(2,1)}, bf16[1,160,512]{2,1,0:T(8,128)(2,1)}, u32[]{:S(2)}, u32[]{:S(2)}) collective-permute-start(bf16[1,160,512]{2,1,0:T(8,128)(2,1)} %get-tuple-element.112), channel_id=1, source_target_pairs={{0,3},{1,0},{2,1},{3,2},{4,7},{5,4},{6,5},{7,6},{8,11},{9,8},{10,9... | collective-permute-start | bytes 491528 | tf_op jit(solution)/shard_map/ppermute | solution.py:365
  386.7 79.7 %collective-permute-start.15 = (bf16[1,160,512]{2,1,0:T(8,128)(2,1)}, bf16[1,160,512]{2,1,0:T(8,128)(2,1)}, u32[]{:S(2)}, u32[]{:S(2)}) collective-permute-start(bf16[1,160,512]{2,1,0:T(8,128)(2,1)} %get-tuple-element.113), channel_id=1, source_target_pairs={{0,2},{1,3},{2,0},{3,1},{4,6},{5,7},{6,4},{7,5},{8,10},{9,11},{10,... | collective-permute-start | bytes 491528 | tf_op jit(solution)/shard_map/ppermute | solution.py:365
  388.3 78.7 %collective-permute-start.14 = (bf16[1,160,512]{2,1,0:T(8,128)(2,1)}, bf16[1,160,512]{2,1,0:T(8,128)(2,1)}, u32[]{:S(2)}, u32[]{:S(2)}) collective-permute-start(bf16[1,160,512]{2,1,0:T(8,128)(2,1)} %get-tuple-element.111), channel_id=1, source_target_pairs={{0,1},{1,2},{2,3},{3,0},{4,5},{5,6},{6,7},{7,4},{8,9},{9,10},{10,1... | collective-permute-start | bytes 491528 | tf_op jit(solution)/shard_map/ppermute | solution.py:365
  439.6 57.2 %collective-permute-start.29 = (bf16[256,2048]{1,0:T(8,128)(2,1)}, bf16[256,2048]{1,0:T(8,128)(2,1)}, u32[]{:S(2)}, u32[]{:S(2)}) collective-permute-start(bf16[256,2048]{1,0:T(8,128)(2,1)} %all-reduce.3.cloned.1.call-done), channel_id=1, source_target_pairs={{0,64},{64,0},{1,65},{65,1},{2,66},{66,2},{3,67},{67,3},{4,68},{68... | collective-permute-start | bytes 3145736 | tf_op jit(solution)/shard_map/ppermute | solution.py:236
  (56 other events, 588.6 us)
Sparse Core Ops, SparseCore 0:
  88.5 38.0 all-gather.1
  327.6 111.9 all-reduce.2
  442.6 46.7 reduce-scatter.1

commit v2 on v0

--- a/solution.py
+++ b/solution.py
@@ -50,7 +50,8 @@
         for m in range(1, radix):
             pairs = [(j + m * stride, j) for j in range(0, count, span) if j + m * stride < count]
             if pairs:
-                total = total + lax.ppermute(block, axis, pairs)
+                sent = lax.ppermute(block.astype(jnp.bfloat16), axis, pairs)
+                total = total + sent.astype(block.dtype)
         block = total
         stride *= radix
     return block

time: 501 us -> 503 us (level)
    ppermute x6, waiting for transfers between devices: 39.3 us -> 48 us  [reduce_to_first(): sent = lax.ppermute(block.astype(jnp.bfloat16), axis, pairs)]
    unnamed x87 -> x91, local copies, waits for them, and re-layouts: 27.7 us -> 27.3 us
  transfers between devices with their start and end apart: 38 -> 38, of which waited for: 14 -> 15; matrix products, arithmetic and copies ran while one was open for 42% -> 39% of each run, Pallas kernels for 0% -> 0%
where the time goes in v2:
time: 503 us; the launch traced here: 494 us
  waiting for transfers between devices  151 us (30%)
  local copies, waits for them, and re-layouts  107 us (21%)
  starting transfers between devices  84.4 us (17%)
  matrix products  71.5 us (14%)
  other arithmetic  64.2 us (13%)
  between operations  15.4 us (3%)
    ppermute x6, waiting for transfers between devices, reduce_to_first(): sent = lax.ppermute(block.astype(jnp.bfloat16), axis, pairs)  48 us
    unnamed x91, local copies, waits for them, and re-layouts  27.3 us
    ppermute x6, waiting for transfers between devices, broadcast_first(): got = lax.ppermute(block, axis, pairs)  26.9 us
    all_to_all x2, waiting for transfers between devices, fetch(): lax.all_to_all(served, 'seq', split_axis=0, concat_axis=0, tiled=True)  26.5 us
    ppermute x6, waiting for transfers between devices, to_owners(): pieces.append(lax.ppermute(sent, 'head', pairs))  17.1 us
    all_to_all x2, starting transfers between devices, fetch(): lax.all_to_all(served, 'seq', split_axis=0, concat_axis=0, tiled=True)  14.9 us
    ppermute x6, starting transfers between devices, broadcast_first(): got = lax.ppermute(block, axis, pairs)  14.6 us
    another operation x4, local copies, waits for them, and re-layouts, per_device(): jnp.stack([pair_view[:block_count], pair_view[1:block_count + 1], pair_vi...  12.4 us
  transfers between devices with their start and end apart: 38, of which 15 were waited for; matrix products, arithmetic and copies ran while one was open for 39% of the time, Pallas kernels for 0%

profile of v2, /device:TPU:1, one launch (start us, length us, event | category | flops | bytes accessed | tf_op | source)
XLA Modules:
  0.0 493.7 jit_solution(5254320306175742358)
XLA Ops:
  14.6 5.3 %reshape.773 = bf16[3,160,4,512]{3,2,1,0:T(4,128)(2,1)} reshape(bf16[3,160,2048]{2,1,0:T(8,128)(2,1)} %pad_maximum_fusion.1) | data formatting | bytes 3932160 | tf_op jit(solution)/shard_map/reshape | solution.py:108
  39.4 11.8 %all-to-all-done = bf16[4,3,160,512]{3,2,1,0:T(8,128)(2,1)} async-done(((bf16[4,3,160,512]{3,2,1,0:T(8,128)(2,1)}), bf16[4,3,160,512]{3,2,1,0:T(8,128)(2,1)}, u32[]{:S(2)}, u32[]{:S(2)}) %all-to-all-start) | async-done | bytes 1966112 | tf_op jit(solution)/shard_map/all_to_all | solution.py:109
  64.3 4.8 pad_maximum_fusion.5
  77.0 9.1 %all-to-all-start.1 = ((bf16[16,15,64,128]{3,2,1,0:T(8,128)(2,1)}), bf16[16,15,64,128]{3,2,1,0:T(8,128)(2,1)}, u32[]{:S(2)}, u32[]{:S(2)}) async-start(bf16[16,15,64,128]{3,2,1,0:T(8,128)(2,1)} %bitcast.361), calls=%async_computation.1 | async-start | bytes 7864320 | tf_op jit(solution)/shard_map/all_to_all | solution.py:149
  88.1 5.1 %collective-permute-start.2 = (bf16[64,1024]{1,0:T(8,128)(2,1)S(1)}, bf16[64,1024]{1,0:T(8,128)(2,1)}, u32[]{:S(2)}, u32[]{:S(2)}) collective-permute-start(bf16[64,1024]{1,0:T(8,128)(2,1)S(1)} %get-tuple-element.108), channel_id=1, source_target_pairs={{0,48},{1,49},{2,50},{3,51},{64,112},{65,113},{66,114},{67,115}} | collective-permute-start | bytes 393224 | tf_op jit(solution)/shard_map/ppermute | solution.py:37
  103.4 26.9 %collective-permute-done.2 = bf16[64,1024]{1,0:T(8,128)(2,1)} collective-permute-done((bf16[64,1024]{1,0:T(8,128)(2,1)S(1)}, bf16[64,1024]{1,0:T(8,128)(2,1)}, u32[]{:S(2)}, u32[]{:S(2)}) %collective-permute-start.2) | collective-permute-done | bytes 131104 | tf_op jit(solution)/shard_map/ppermute | solution.py:37
  143.7 4.9 pad_maximum_fusion
  156.3 5.8 %all-to-all-start.2 = ((bf16[16,15,64,128]{3,2,1,0:T(8,128)(2,1)}), bf16[16,15,64,128]{3,2,1,0:T(8,128)(2,1)}, u32[]{:S(2)}, u32[]{:S(2)}) async-start(bf16[16,15,64,128]{3,2,1,0:T(8,128)(2,1)} %bitcast.366), calls=%async_computation.2 | async-start | bytes 7864320 | tf_op jit(solution)/shard_map/all_to_all | solution.py:149
  162.1 5.0 %select_reduce_fusion = (f32[4,10,64]{2,1,0:T(8,128)}, f32[4,10,64,192]{3,2,1,0:T(8,128)}) fusion(pred[10,192]{1,0:T(8,128)(4,1)S(1)} %broadcast_in_dim.121, bf16[10,192,2,4,128]{4,1,0,3,2:T(8,128)(2,1)} %bitcast.364, bf16[10,64,4,128]{3,2,1,0:T(4,128)(2,1)S(1)} %reshape_squeeze.2), kind=kOutput, calls=%fused_computation.67 | convolution fusion | flops 127301120 | bytes 4599680 | tf_op jit(solution)/shard_map/ibhd,ikhd->hibk/dot_general | solution.py:173
  176.6 4.8 fusion.52
  191.8 26.5 %all-to-all-done.2 = bf16[16,15,64,128]{3,2,1,0:T(8,128)(2,1)} async-done(((bf16[16,15,64,128]{3,2,1,0:T(8,128)(2,1)}), bf16[16,15,64,128]{3,2,1,0:T(8,128)(2,1)}, u32[]{:S(2)}, u32[]{:S(2)}) %all-to-all-start.2) | async-done | bytes 3932192 | tf_op jit(solution)/shard_map/all_to_all | solution.py:149
  218.3 5.0 %fusion.55 = bf16[20,8,64,128]{3,1,2,0:T(8,128)(2,1)S(1)} fusion(bf16[30,8,64,128]{3,2,1,0:T(8,128)(2,1)} %bitcast.154, s32[160]{0:T(256)S(1)} %convert_add_fusion.2), kind=kOutput, calls=%fused_computation.87 | convolution fusion | flops 630494720 | bytes 6554240 | tf_op jit(solution)/shard_map/dot_general | solution.py:150
  287.7 4.7 fusion.21
  292.4 4.9 fusion.19
  304.9 5.1 %all-to-all-start.3 = ((bf16[16,15,64,128]{3,2,1,0:T(8,128)(2,1)}), bf16[16,15,64,128]{3,2,1,0:T(8,128)(2,1)}, u32[]{:S(2)}, u32[]{:S(2)}) async-start(bf16[16,15,64,128]{3,2,1,0:T(8,128)(2,1)} %bitcast.362), calls=%async_computation.4 | async-start | bytes 7864320 | tf_op jit(solution)/shard_map/all_to_all | solution.py:344
  321.3 41.6 %collective-permute-done.19 = bf16[64,1024]{1,0:T(8,128)(2,1)} collective-permute-done((bf16[64,1024]{1,0:T(8,128)(2,1)}, bf16[64,1024]{1,0:T(8,128)(2,1)}, u32[]{:S(2)}, u32[]{:S(2)}) %collective-permute-start.19) | collective-permute-done | bytes 131104 | tf_op jit(solution)/shard_map/ppermute | solution.py:53
  362.9 6.4 %collective-permute-done.18 = bf16[64,1024]{1,0:T(8,128)(2,1)} collective-permute-done((bf16[64,1024]{1,0:T(8,128)(2,1)}, bf16[64,1024]{1,0:T(8,128)(2,1)}, u32[]{:S(2)}, u32[]{:S(2)}) %collective-permute-start.18) | collective-permute-done | bytes 131104 | tf_op jit(solution)/shard_map/ppermute | solution.py:53
  388.3 4.6 collective-permute-start.23
  412.9 10.0 %all-reduce.3.cloned.1.call-done = bf16[256,2048]{1,0:T(8,128)(2,1)} async-done(((bf16[256,2048]{1,0:T(8,128)(2,1)}), bf16[256,2048]{1,0:T(8,128)(2,1)}) %all-reduce.3.cloned.1.call-update) | async-done | bytes 1048592 | tf_op jit(solution)/shard_map/psum | solution.py:235
  428.1 5.9 %fusion.59 = f32[10,4,64,1,128]{4,0,2,1,3:T(8,128)} fusion(s32[10,4]{0,1:T(4,128)S(1)} %copy-done.38, s32[240]{0:T(256)S(1)} %sub.182, bf16[30,8,64,128]{3,2,1,0:T(8,128)(2,1)} %bitcast.178), kind=kOutput, calls=%fused_computation.94 | convolution fusion | flops 157296000 | bytes 5244000 | tf_op jit(solution)/shard_map/dot_general | solution.py:345
  434.0 5.2 %fusion.58 = f32[10,4,64,1,128]{4,0,2,1,3:T(8,128)S(1)} fusion(s32[10,4]{0,1:T(4,128)S(1)} %copy-done.38, s32[240]{0:T(256)S(1)} %sub.182, bf16[30,8,64,128]{3,2,1,0:T(8,128)(2,1)} %bitcast.169), kind=kOutput, calls=%fused_computation.93 | convolution fusion | flops 157296000 | bytes 5244000 | tf_op jit(solution)/shard_map/dot_general | solution.py:345
  456.6 8.9 %collective-permute-done.27 = bf16[2,160,512]{2,1,0:T(8,128)(2,1)} collective-permute-done((bf16[2,160,512]{2,1,0:T(8,128)(2,1)}, bf16[2,160,512]{2,1,0:T(8,128)(2,1)}, u32[]{:S(2)}, u32[]{:S(2)}) %collective-permute-start.27) | collective-permute-done | bytes 327712 | tf_op jit(solution)/shard_map/ppermute | solution.py:367
  466.9 6.8 %collective-permute-done.25 = bf16[2,160,512]{2,1,0:T(8,128)(2,1)} collective-permute-done((bf16[2,160,512]{2,1,0:T(8,128)(2,1)}, bf16[2,160,512]{2,1,0:T(8,128)(2,1)}, u32[]{:S(2)}, u32[]{:S(2)}) %collective-permute-start.25) | collective-permute-done | bytes 327712 | tf_op jit(solution)/shard_map/ppermute | solution.py:367
  480.1 6.6 %maximum_select_fusion = f32[512,2048]{1,0:T(8,128)} fusion(f32[256,2048]{1,0:T(8,128)} %collective-permute-done.29, f32[256,2048]{1,0:T(8,128)} %convert_multiply_fusion, pred[]{:T(512)S(6)} %eq.179), kind=kLoop, calls=%fused_computation.20 | loop fusion | flops 3145728 | bytes 8388609 | tf_op jit(solution)/shard_map/jit(_where)/select_n | solution.py:239
  (310 shorter events, 252.6 us)
Async XLA Ops:
  7.2 21.4 %collective-permute-start.10 = (s32[10,4,4]{0,2,1:T(4,128)}, s32[10,4,4]{0,2,1:T(4,128)S(1)}, u32[]{:S(2)}, u32[]{:S(2)}) collective-permute-start(s32[10,4,4]{0,2,1:T(4,128)} %param.21), channel_id=1, source_target_pairs={{0,12},{4,0},{8,4},{12,8},{16,28},{20,16},{24,20},{28,24},{32,44},... | collective-permute-start | bytes 1928 | tf_op jit(solution)/shard_map/ppermute | solution.py:90
  23.1 28.1 %all-to-all-start = ((bf16[4,3,160,512]{3,2,1,0:T(8,128)(2,1)}), bf16[4,3,160,512]{3,2,1,0:T(8,128)(2,1)}, u32[]{:S(2)}, u32[]{:S(2)}) async-start(bf16[4,3,160,512]{3,2,1,0:T(8,128)(2,1)} %copy.354), calls=%async_computation | async-start | bytes 3932160 | tf_op jit(solution)/shard_map/all_to_all | solution.py:109
  77.0 79.3 %all-to-all-start.1 = ((bf16[16,15,64,128]{3,2,1,0:T(8,128)(2,1)}), bf16[16,15,64,128]{3,2,1,0:T(8,128)(2,1)}, u32[]{:S(2)}, u32[]{:S(2)}) async-start(bf16[16,15,64,128]{3,2,1,0:T(8,128)(2,1)} %bitcast.361), calls=%async_computation.1 | async-start | bytes 7864320 | tf_op jit(solution)/shard_map/all_to_all | solution.py:149
  86.0 84.6 %all-gather.2.cloned.1.call-start = ((), (), s32[]{:S(2)}) async-start(), calls=%async_computation.7 | async-start | bytes 3276800 | tf_op jit(solution)/shard_map/all_gather | solution.py:224
  88.1 42.2 %collective-permute-start.2 = (bf16[64,1024]{1,0:T(8,128)(2,1)S(1)}, bf16[64,1024]{1,0:T(8,128)(2,1)}, u32[]{:S(2)}, u32[]{:S(2)}) collective-permute-start(bf16[64,1024]{1,0:T(8,128)(2,1)S(1)} %get-tuple-element.108), channel_id=1, source_target_pairs={{0,48},{1,49},{2,50},{3,51},{64,112},{65,113},{66,114},{67,115}} | collective-permute-start | bytes 393224 | tf_op jit(solution)/shard_map/ppermute | solution.py:37
  93.2 37.1 %collective-permute-start.3 = (bf16[64,1024]{1,0:T(8,128)(2,1)S(1)}, bf16[64,1024]{1,0:T(8,128)(2,1)}, u32[]{:S(2)}, u32[]{:S(2)}) collective-permute-start(bf16[64,1024]{1,0:T(8,128)(2,1)S(1)} %get-tuple-element.108), channel_id=1, source_target_pairs={{0,32},{1,33},{2,34},{3,35},{64,96},{65,97},{66,98},{67,99}} | collective-permute-start | bytes 393224 | tf_op jit(solution)/shard_map/ppermute | solution.py:37
  95.2 35.2 %collective-permute-start.4 = (bf16[64,1024]{1,0:T(8,128)(2,1)S(1)}, bf16[64,1024]{1,0:T(8,128)(2,1)}, u32[]{:S(2)}, u32[]{:S(2)}) collective-permute-start(bf16[64,1024]{1,0:T(8,128)(2,1)S(1)} %get-tuple-element.108), channel_id=1, source_target_pairs={{0,16},{1,17},{2,18},{3,19},{64,80},{65,81},{66,82},{67,83}} | collective-permute-start | bytes 393224 | tf_op jit(solution)/shard_map/ppermute | solution.py:37
  131.0 36.1 %collective-permute-start.5 = (bf16[64,1024]{1,0:T(8,128)(2,1)}, bf16[64,1024]{1,0:T(8,128)(2,1)S(1)}, u32[]{:S(2)}, u32[]{:S(2)}) collective-permute-start(bf16[64,1024]{1,0:T(8,128)(2,1)} %select_select_fusion.1), channel_id=1, source_target_pairs={{0,12},{16,28},{32,44},{48,60},{1,13},{17,29},{33,45},{49,61},{2,1... | collective-permute-start | bytes 393224 | tf_op jit(solution)/shard_map/ppermute | solution.py:37
  132.3 34.8 %collective-permute-start.6 = (bf16[64,1024]{1,0:T(8,128)(2,1)}, bf16[64,1024]{1,0:T(8,128)(2,1)}, u32[]{:S(2)}, u32[]{:S(2)}) collective-permute-start(bf16[64,1024]{1,0:T(8,128)(2,1)} %select_select_fusion.1), channel_id=1, source_target_pairs={{0,8},{16,24},{32,40},{48,56},{1,9},{17,25},{33,41},{49,57},{2,10}... | collective-permute-start | bytes 393224 | tf_op jit(solution)/shard_map/ppermute | solution.py:37
  134.2 32.9 %collective-permute-start.7 = (bf16[64,1024]{1,0:T(8,128)(2,1)}, bf16[64,1024]{1,0:T(8,128)(2,1)}, u32[]{:S(2)}, u32[]{:S(2)}) collective-permute-start(bf16[64,1024]{1,0:T(8,128)(2,1)} %select_select_fusion.1), channel_id=1, source_target_pairs={{0,4},{16,20},{32,36},{48,52},{1,5},{17,21},{33,37},{49,53},{2,6},... | collective-permute-start | bytes 393224 | tf_op jit(solution)/shard_map/ppermute | solution.py:37
  156.3 62.0 %all-to-all-start.2 = ((bf16[16,15,64,128]{3,2,1,0:T(8,128)(2,1)}), bf16[16,15,64,128]{3,2,1,0:T(8,128)(2,1)}, u32[]{:S(2)}, u32[]{:S(2)}) async-start(bf16[16,15,64,128]{3,2,1,0:T(8,128)(2,1)} %bitcast.366), calls=%async_computation.2 | async-start | bytes 7864320 | tf_op jit(solution)/shard_map/all_to_all | solution.py:149
  247.4 57.6 %all-to-all-start.4 = ((bf16[16,15,64,128]{3,2,1,0:T(8,128)(2,1)}), bf16[16,15,64,128]{3,2,1,0:T(8,128)(2,1)}, u32[]{:S(2)}, u32[]{:S(2)}) async-start(bf16[16,15,64,128]{3,2,1,0:T(8,128)(2,1)} %bitcast.367), calls=%async_computation.5 | async-start | bytes 7864320 | tf_op jit(solution)/shard_map/all_to_all | solution.py:344
  251.9 171.0 %all-reduce.3.cloned.1.call-start = ((), (), s32[]{:S(2)}) async-start(), calls=%async_computation.8 | async-start | bytes 2097152 | tf_op jit(solution)/shard_map/psum | solution.py:235
  267.2 30.1 %collective-permute-start.28 = (f32[256,2048]{1,0:T(8,128)}, f32[256,2048]{1,0:T(8,128)}, u32[]{:S(2)}, u32[]{:S(2)}) collective-permute-start(f32[256,2048]{1,0:T(8,128)} %constant_dynamic-slice_fusion), channel_id=1, source_target_pairs={{0,64},{64,0},{1,65},{65,1},{2,66},{66,2},{3,67},{67,3},{4,68},{68... | collective-permute-start | bytes 6291464 | tf_op jit(solution)/shard_map/ppermute | solution.py:234
  304.9 129.0 %all-to-all-start.3 = ((bf16[16,15,64,128]{3,2,1,0:T(8,128)(2,1)}), bf16[16,15,64,128]{3,2,1,0:T(8,128)(2,1)}, u32[]{:S(2)}, u32[]{:S(2)}) async-start(bf16[16,15,64,128]{3,2,1,0:T(8,128)(2,1)} %bitcast.362), calls=%async_computation.4 | async-start | bytes 7864320 | tf_op jit(solution)/shard_map/all_to_all | solution.py:344
  310.1 176.6 %reduce-scatter.2.cloned.1.call-start = ((), (), s32[]{:S(2)}) async-start(), calls=%async_computation.6 | async-start | bytes 3276800 | tf_op jit(solution)/shard_map/reduce_scatter | solution.py:218
  311.2 51.7 %collective-permute-start.19 = (bf16[64,1024]{1,0:T(8,128)(2,1)}, bf16[64,1024]{1,0:T(8,128)(2,1)}, u32[]{:S(2)}, u32[]{:S(2)}) collective-permute-start(bf16[64,1024]{1,0:T(8,128)(2,1)} %convert_element_type.197), channel_id=1, source_target_pairs={{12,0},{28,16},{44,32},{60,48},{13,1},{29,17},{45,33},{61,49},{14,... | collective-permute-start | bytes 393224 | tf_op jit(solution)/shard_map/ppermute | solution.py:53
  312.6 56.6 %collective-permute-start.18 = (bf16[64,1024]{1,0:T(8,128)(2,1)}, bf16[64,1024]{1,0:T(8,128)(2,1)}, u32[]{:S(2)}, u32[]{:S(2)}) collective-permute-start(bf16[64,1024]{1,0:T(8,128)(2,1)} %convert_element_type.197), channel_id=1, source_target_pairs={{8,0},{24,16},{40,32},{56,48},{9,1},{25,17},{41,33},{57,49},{10,2}... | collective-permute-start | bytes 393224 | tf_op jit(solution)/shard_map/ppermute | solution.py:53
  313.9 55.3 %collective-permute-start.17 = (bf16[64,1024]{1,0:T(8,128)(2,1)}, bf16[64,1024]{1,0:T(8,128)(2,1)}, u32[]{:S(2)}, u32[]{:S(2)}) collective-permute-start(bf16[64,1024]{1,0:T(8,128)(2,1)} %convert_element_type.197), channel_id=1, source_target_pairs={{4,0},{20,16},{36,32},{52,48},{5,1},{21,17},{37,33},{53,49},{6,2},... | collective-permute-start | bytes 393224 | tf_op jit(solution)/shard_map/ppermute | solution.py:53
  393.7 58.9 %collective-permute-start.16 = (bf16[1,160,512]{2,1,0:T(8,128)(2,1)}, bf16[1,160,512]{2,1,0:T(8,128)(2,1)}, u32[]{:S(2)}, u32[]{:S(2)}) collective-permute-start(bf16[1,160,512]{2,1,0:T(8,128)(2,1)} %get-tuple-element.110), channel_id=1, source_target_pairs={{0,3},{1,0},{2,1},{3,2},{4,7},{5,4},{6,5},{7,6},{8,11},{9,8},{10,9... | collective-permute-start | bytes 491528 | tf_op jit(solution)/shard_map/ppermute | solution.py:367
  395.2 57.9 %collective-permute-start.15 = (bf16[1,160,512]{2,1,0:T(8,128)(2,1)}, bf16[1,160,512]{2,1,0:T(8,128)(2,1)}, u32[]{:S(2)}, u32[]{:S(2)}) collective-permute-start(bf16[1,160,512]{2,1,0:T(8,128)(2,1)} %get-tuple-element.111), channel_id=1, source_target_pairs={{0,2},{1,3},{2,0},{3,1},{4,6},{5,7},{6,4},{7,5},{8,10},{9,11},{10,... | collective-permute-start | bytes 491528 | tf_op jit(solution)/shard_map/ppermute | solution.py:367
  396.5 57.2 %collective-permute-start.14 = (bf16[1,160,512]{2,1,0:T(8,128)(2,1)}, bf16[1,160,512]{2,1,0:T(8,128)(2,1)}, u32[]{:S(2)}, u32[]{:S(2)}) collective-permute-start(bf16[1,160,512]{2,1,0:T(8,128)(2,1)} %get-tuple-element.109), channel_id=1, source_target_pairs={{0,1},{1,2},{2,3},{3,0},{4,5},{5,6},{6,7},{7,4},{8,9},{9,10},{10,1... | collective-permute-start | bytes 491528 | tf_op jit(solution)/shard_map/ppermute | solution.py:367
  425.8 54.4 %collective-permute-start.29 = (f32[256,2048]{1,0:T(8,128)}, f32[256,2048]{1,0:T(8,128)}, u32[]{:S(2)}, u32[]{:S(2)}) collective-permute-start(f32[256,2048]{1,0:T(8,128)} %convert_multiply_fusion), channel_id=1, source_target_pairs={{0,64},{64,0},{1,65},{65,1},{2,66},{66,2},{3,67},{67,3},{4,68},{68... | collective-permute-start | bytes 6291464 | tf_op jit(solution)/shard_map/ppermute | solution.py:238
  453.2 20.5 %collective-permute-start.25 = (bf16[2,160,512]{2,1,0:T(8,128)(2,1)}, bf16[2,160,512]{2,1,0:T(8,128)(2,1)}, u32[]{:S(2)}, u32[]{:S(2)}) collective-permute-start(bf16[2,160,512]{2,1,0:T(8,128)(2,1)} %get-tuple-element.101), channel_id=1, source_target_pairs={{0,1},{1,2},{2,3},{3,0},{4,5},{5,6},{6,7},{7,4},{8,9},{9,10},{10,1... | collective-permute-start | bytes 983048 | tf_op jit(solution)/shard_map/ppermute | solution.py:367
  (55 other events, 527.6 us)
Sparse Core Ops, SparseCore 0:
  88.5 38.0 all-gather.1
  300.3 122.5 all-reduce.2
  425.9 43.4 reduce-scatter.1
